TPU v7x, 128 devices: a whole 4x4x4 slice. The times are simulated.
128 devices in a mesh: sector: 8 (over y, core), row: 16 (over x, z).
Axes of the slice: x: 4, y: 4, z: 4, core: 2. Of those that a mesh axis runs over, the one named last changes fastest.
Arguments:
- amplitudes: bfloat16 [8192, 4, 8192], P('sector', None, 'row'), may hold values from -6 to 6
- next_site: bfloat16 [8, 4, 8192, 2048], P('sector', None, 'row'), may hold values from -0.03125 to 0.03125
- sector_rows: int32 [8], replicated, may hold values from 512 to 1024, as said below
- moves: int32 [2, 8], replicated, may hold values from 0 to 128, as said below
- angles: float32 [2, 8, 128], replicated, may hold values from -3.140625 to 3.140625
- ranks: int32 [8], replicated, may hold values from 256 to 1024, as said below
Outputs:
- canonical: bfloat16 [2048, 8192], P('row', 'sector')
Inputs may be any that keep to these rules, and one draw needn't show every extreme that they name: `sector_rows`: one sector has exactly 1024 live rows and another exactly 512. `moves`: the entry of the last sector is 0, every other entry is 1 or more; for each gate some pair moves exactly 128 rows. `ranks`: each sector keeps at least half of its live rows and at most all of them; one sector keeps 1024 rows and one keeps 1024 // 4.
All inputs are finite; a program needn't handle non-finite values.
Results may differ from a plain program's by a relative error of at most 0.014.
Values may be sent and summed in bfloat16 or wider, within the bound.
No kernel may reach another device: no remote copies, remote signals or barrier semaphores. Data moves between devices by JAX's collectives and lax.ppermute only.
A program may use at most 128 MiB of HBM per device.

v0:
```python
import math
import jax
import jax.numpy as jnp
from jax import lax
from jax.sharding import PartitionSpec as P

KOUT = 2048


def shifted(x, axis, by):
    size = lax.axis_size(axis)
    pairs = [(i, i + by) for i in range(size) if 0 <= i + by < size]
    return lax.ppermute(x, axis, pairs)


def rotate_rows(
    padded, start_a, start_b, from_above, from_below, angle_here, angle_prev, count_here, count_prev
):
    slot_count = from_above.shape[0]
    slot_index = jnp.arange(slot_count)
    rows_a = lax.dynamic_slice_in_dim(padded, start_a, slot_count, 0)
    rows_b = lax.dynamic_slice_in_dim(padded, start_b, slot_count, 0)
    above_rows = from_above.astype(jnp.float32)
    below_rows = from_below.astype(jnp.float32)
    cos_here = jnp.cos(angle_here)[:, None, None]
    sin_here = jnp.sin(angle_here)[:, None, None]
    cos_prev = jnp.cos(angle_prev)[:, None, None]
    sin_prev = jnp.sin(angle_prev)[:, None, None]
    new_a = jnp.where(
        (slot_index < count_here)[:, None, None], cos_here * rows_a - sin_here * above_rows, rows_a
    )
    new_b = jnp.where(
        (slot_index < count_prev)[:, None, None], sin_prev * below_rows + cos_prev * rows_b, rows_b
    )
    padded = lax.dynamic_update_slice_in_dim(padded, new_a, start_a, 0)
    return lax.dynamic_update_slice_in_dim(padded, new_b, start_b, 0)


def per_device(amplitudes, next_site, sector_rows, moves, angles, ranks):
    sector_id = lax.axis_index("sector")
    sector_rows_count = amplitudes.shape[0]
    move_rows = sector_rows_count // 8
    row_index = jnp.arange(sector_rows_count)
    live_rows = sector_rows[sector_id]
    prev_id = jnp.maximum(sector_id - 1, 0)
    count_here = moves[:, sector_id]
    count_prev = jnp.where(sector_id > 0, moves[:, prev_id], 0)
    local_rows = jnp.where(
        (row_index < live_rows)[:, None, None], amplitudes.astype(jnp.float32), 0.0
    )
    tail_zeros = jnp.zeros((move_rows,) + local_rows.shape[1:], jnp.float32)
    padded = jnp.concatenate([local_rows, tail_zeros], 0)
    starts_a = [live_rows - count_here[0], live_rows - count_here[0] - count_here[1]]
    starts_b = [jnp.int32(0), count_prev[0]]
    for gate_index in range(2):
        send_up = lax.dynamic_slice_in_dim(padded, starts_a[gate_index], move_rows, 0).astype(
            jnp.bfloat16
        )
        send_down = lax.dynamic_slice_in_dim(padded, starts_b[gate_index], move_rows, 0).astype(
            jnp.bfloat16
        )
        from_below = shifted(send_up, "sector", 1)
        from_above = shifted(send_down, "sector", -1)
        padded = rotate_rows(
            padded,
            starts_a[gate_index],
            starts_b[gate_index],
            from_above,
            from_below,
            angles[gate_index][sector_id],
            angles[gate_index][prev_id],
            count_here[gate_index],
            count_prev[gate_index],
        )
    block_rows = padded[:sector_rows_count].astype(jnp.bfloat16)
    site_tensor = next_site[0]
    contracted = lax.psum_scatter(
        jnp.einsum("prk,lpr->kl", site_tensor, block_rows, preferred_element_type=jnp.float32),
        "row",
        scatter_dimension=0,
        tiled=True,
    ).astype(jnp.bfloat16)
    local_gram = lax.dot_general(
        contracted, contracted, (((0,), (0,)), ((), ())), preferred_element_type=jnp.float32
    )
    gram_matrix = lax.psum(local_gram, "row")
    dead_rows = (row_index >= live_rows).astype(jnp.float32)
    gram_matrix = gram_matrix + jnp.diag(dead_rows)
    factor_low = jnp.linalg.cholesky(gram_matrix)
    solved = jax.scipy.linalg.solve_triangular(
        factor_low, contracted.astype(jnp.float32).T, lower=True
    ).T
    kept_mask = ((row_index >= live_rows - ranks[sector_id]) & (row_index < live_rows)).astype(
        jnp.float32
    )
    return (solved * math.sqrt(KOUT) * kept_mask[None, :]).astype(jnp.bfloat16)


def solution(mesh):
    placed = (P("sector", None, "row"), P("sector", None, "row", None), P(), P(), P(), P())
    return jax.shard_map(
        per_device, mesh=mesh, in_specs=placed, out_specs=P("row", "sector"), check_vma=False
    )
```

profile of v0, /device:TPU:1, one launch (start us, length us, event | category | flops | bytes accessed | tf_op | source)
XLA Modules:
  0.0 640.3 jit_solution(2084765456773674766)
XLA Ops:
  11.0 3.8 convert_select_fusion
  15.2 3.1 copy-done
  18.2 3.3 collective-permute-start
  21.5 3.2 collective-permute-start.1
  27.3 8.1 %concatenate.30 = f32[1152,4,512]{2,0,1:T(8,128)} pad(f32[1024,4,512]{2,0,1:T(8,128)} %copy-done, f32[]{:T(128)} %constant.290.clone.1), padding=0_128x0_0x0_0 | pad | bytes 17825796 | tf_op jit(solution)/shard_map/concatenate | solution.py:52
  36.8 1.6 subtract_select_fusion.1
  38.4 5.9 dynamic_update_slice.12
  44.3 2.5 select_dynamic-update-slice_fusion
  46.8 1.9 dynamic-slice_convert_fusion.1
  48.7 1.9 collective-permute-start.2
  50.6 3.6 collective-permute-start.3
  55.6 3.5 collective-permute-done.2
  60.4 2.2 add_select_fusion
  62.6 5.9 dynamic_update_slice.14
  68.5 5.9 dynamic_update_slice.15
  74.4 15.6 %fusion.2 = f32[2048,1024]{0,1:T(8,128)} fusion(bf16[1,4,512,2048]{3,2,1,0:T(8,128)(2,1)} %param.7, f32[1152,4,512]{2,0,1:T(8,128)} %dynamic_update_slice.15), kind=kOutput, calls=%fused_computation.7 | convolution fusion | flops 8589934592 | bytes 20971520 | tf_op jit(solution)/shard_map/prk,lpr->kl/dot_general | solution.py:78
  90.1 87.1 %reduce-scatter.2.cloned.1.call-done = f32[128,1024]{0,1:T(8,128)} async-done(((f32[2048,1024]{0,1:T(8,128)}), f32[128,1024]{0,1:T(8,128)}) %reduce-scatter.2.cloned.1.call-update) | async-done | bytes 524304 | tf_op jit(solution)/shard_map/reduce_scatter | solution.py:77
  177.2 3.9 fusion.46
  184.3 100.9 %all-reduce.4.cloned.1.call-done = f32[1024,1024]{0,1:T(8,128)} async-done(((f32[1024,1024]{0,1:T(8,128)}), f32[1024,1024]{0,1:T(8,128)}) %all-reduce.4.cloned.1.call-update) | async-done | bytes 4194320 | tf_op jit(solution)/shard_map/psum | solution.py:86
  285.2 4.8 select_add_fusion
  290.0 5.8 copy.9
  295.8 4.4 fusion.5
  300.3 1.9 copy-done.1
  302.2 11.7 %cholesky.222 = f32[128,128]{1,0:T(8,128)S(1)} custom-call(f32[128,128]{1,0:T(8,128)S(1)} %cholesky.577), custom_call_target="Cholesky" | custom-call | tf_op jit(solution)/shard_map/jit(cholesky)/cholesky | solution.py:89
  314.0 9.8 %custom-call.63 = f32[1,128,128]{1,2,0:T(8,128)S(1)} custom-call(f32[1,128,128]{2,1,0:T(8,128)S(1)} %get-tuple-element.73), custom_call_target="InvertDiagBlocksLowerTriangular" | custom-call | tf_op jit(solution)/shard_map/jit(cholesky)/cholesky | solution.py:89
  323.8 1.5 fusion.13
  325.3 1.6 convolution_subtract_fusion
  326.9 11.7 %cholesky.243 = f32[128,128]{1,0:T(8,128)S(1)} custom-call(f32[128,128]{1,0:T(8,128)S(1)} %cholesky.581), custom_call_target="Cholesky" | custom-call | tf_op jit(solution)/shard_map/jit(cholesky)/cholesky | solution.py:89
  339.2 2.5 cholesky.254
  341.7 9.8 %custom-call.64 = f32[1,128,128]{1,2,0:T(8,128)S(1)} custom-call(f32[1,128,128]{2,1,0:T(8,128)S(1)} %get-tuple-element.71), custom_call_target="InvertDiagBlocksLowerTriangular" | custom-call | tf_op jit(solution)/shard_map/jit(cholesky)/cholesky | solution.py:89
  353.0 1.3 convolution_dynamic-update-slice_fusion
  354.3 2.7 convolution_subtract_fusion.1
  357.0 11.7 %cholesky.466 = f32[128,128]{1,0:T(8,128)S(1)} custom-call(f32[128,128]{1,0:T(8,128)S(1)} %cholesky.586), custom_call_target="Cholesky" | custom-call | tf_op jit(solution)/shard_map/jit(cholesky)/cholesky | solution.py:89
  369.5 9.8 %custom-call.65 = f32[1,128,128]{1,2,0:T(8,128)S(1)} custom-call(f32[1,128,128]{2,1,0:T(8,128)S(1)} %get-tuple-element.69), custom_call_target="InvertDiagBlocksLowerTriangular" | custom-call | tf_op jit(solution)/shard_map/jit(cholesky)/cholesky | solution.py:89
  380.6 3.3 convolution_subtract_fusion.2
  383.9 11.7 %cholesky.485 = f32[128,128]{1,0:T(8,128)S(1)} custom-call(f32[128,128]{1,0:T(8,128)S(1)} %cholesky.591), custom_call_target="Cholesky" | custom-call | tf_op jit(solution)/shard_map/jit(cholesky)/cholesky | solution.py:89
  396.4 9.8 %custom-call.66 = f32[1,128,128]{1,2,0:T(8,128)S(1)} custom-call(f32[1,128,128]{2,1,0:T(8,128)S(1)} %get-tuple-element.67), custom_call_target="InvertDiagBlocksLowerTriangular" | custom-call | tf_op jit(solution)/shard_map/jit(cholesky)/cholesky | solution.py:89
  407.3 3.1 convolution_subtract_fusion.3
  410.5 12.1 %cholesky.504 = f32[128,128]{1,0:T(8,128)S(1)} custom-call(f32[128,128]{1,0:T(8,128)S(1)} %cholesky.596), custom_call_target="Cholesky" | custom-call | tf_op jit(solution)/shard_map/jit(cholesky)/cholesky | solution.py:89
  423.4 9.8 %custom-call.67 = f32[1,128,128]{1,2,0:T(8,128)S(1)} custom-call(f32[1,128,128]{2,1,0:T(8,128)S(1)} %get-tuple-element.65), custom_call_target="InvertDiagBlocksLowerTriangular" | custom-call | tf_op jit(solution)/shard_map/jit(cholesky)/cholesky | solution.py:89
  434.3 3.1 convolution_subtract_fusion.4
  437.4 11.7 %cholesky.524 = f32[128,128]{1,0:T(8,128)S(1)} custom-call(f32[128,128]{1,0:T(8,128)S(1)} %cholesky.601), custom_call_target="Cholesky" | custom-call | tf_op jit(solution)/shard_map/jit(cholesky)/cholesky | solution.py:89
  449.9 9.8 %custom-call.68 = f32[1,128,128]{1,2,0:T(8,128)S(1)} custom-call(f32[1,128,128]{2,1,0:T(8,128)S(1)} %get-tuple-element.63), custom_call_target="InvertDiagBlocksLowerTriangular" | custom-call | tf_op jit(solution)/shard_map/jit(cholesky)/cholesky | solution.py:89
  460.7 2.8 convolution_subtract_fusion.5
  463.5 11.7 %cholesky.544 = f32[128,128]{1,0:T(8,128)S(1)} custom-call(f32[128,128]{1,0:T(8,128)S(1)} %cholesky.606), custom_call_target="Cholesky" | custom-call | tf_op jit(solution)/shard_map/jit(cholesky)/cholesky | solution.py:89
  476.0 9.8 %custom-call.69 = f32[1,128,128]{1,2,0:T(8,128)S(1)} custom-call(f32[1,128,128]{2,1,0:T(8,128)S(1)} %get-tuple-element.61), custom_call_target="InvertDiagBlocksLowerTriangular" | custom-call | tf_op jit(solution)/shard_map/jit(cholesky)/cholesky | solution.py:89
  486.8 2.1 convolution_subtract_fusion.11
  488.9 11.7 %cholesky.562 = f32[128,128]{1,0:T(8,128)S(1)} custom-call(f32[128,128]{1,0:T(8,128)S(1)} %convolution_subtract_fusion.11), custom_call_target="Cholesky" | custom-call | tf_op jit(solution)/shard_map/jit(cholesky)/cholesky | solution.py:89
  511.7 4.8 select_select_fusion
  516.5 23.7 %while.1 = (s32[]{:T(128)}, f32[1024,1024]{0,1:T(8,128)}, s32[8,2]{0,1:T(2,128)S(1)}, f32[8,128,128]{2,1,0:T(8,128)S(1)}, s32[]{:T(128)}) while((s32[]{:T(128)}, f32[1024,1024]{0,1:T(8,128)}, s32[8,2]{0,1:T(2,128)S(1)}, f32[8,128,128]{2,1,0:T(8,128)S(1)}, s32[]{:T(128)}) %tuple.65), condition=%wide.while_cond, body=%wide.while_body.sunk | while | flops 2 | bytes 393321 | solution.py:90
  517.1 2.2 dynamic-slice.11
  520.1 2.2 dynamic-slice.11
  523.1 2.2 dynamic-slice.11
  526.1 2.2 dynamic-slice.11
  529.0 2.2 dynamic-slice.11
  532.0 2.2 dynamic-slice.11
  535.0 2.2 dynamic-slice.11
  538.0 2.2 dynamic-slice.11
  540.3 78.8 %custom-call.70 = f32[8,128,128]{1,2,0:T(8,128)S(1)} custom-call(f32[8,128,128]{2,1,0:T(8,128)S(1)} %get-tuple-element.12), custom_call_target="InvertDiagBlocksLowerTriangular" | custom-call | tf_op jit(solution)/shard_map/jit(_solve_triangular)/triangular_solve | solution.py:90
  622.4 1.4 convolution_subtract_fusion.13
  624.1 1.5 convolution_subtract_fusion.12
  625.9 1.7 convolution_subtract_fusion.8
  627.9 1.8 convolution_subtract_fusion.7
  630.0 1.9 convolution_subtract_fusion.6
  (123 shorter events, 38.3 us)
Async XLA Ops:
  6.5 170.7 %reduce-scatter.2.cloned.1.call-start = ((), (), s32[]{:S(2)}) async-start(), calls=%async_computation.1 | async-start | bytes 8912896 | tf_op jit(solution)/shard_map/reduce_scatter | solution.py:77
  14.9 3.3 copy-start
  14.9 9.8 %copy-start.3 = (f32[2,8,128]{2,1,0:T(8,128)S(1)}, f32[2,8,128]{2,1,0:T(8,128)}, u32[]{:S(2)}) copy-start(f32[2,8,128]{2,1,0:T(8,128)} %param.10) | copy-start | bytes 24580
  18.2 18.6 %collective-permute-start = (bf16[128,4,512]{2,0,1:T(8,128)(2,1)S(1)}, bf16[128,4,512]{2,0,1:T(8,128)(2,1)S(1)}, u32[]{:S(2)}, u32[]{:S(2)}) collective-permute-start(bf16[128,4,512]{2,0,1:T(8,128)(2,1)S(1)} %get-tuple-element.34), channel_id=1, source_target_pairs={{16,0},{32,16},{48,32},{64,48},{80,64},{96,80},{112,96},{17,1},{33... | collective-permute-start | bytes 1572872 | tf_op jit(solution)/shard_map/ppermute | solution.py:13
  21.5 22.8 %collective-permute-start.1 = (bf16[128,4,512]{2,0,1:T(8,128)(2,1)S(1)}, bf16[128,4,512]{2,0,1:T(8,128)(2,1)S(1)}, u32[]{:S(2)}, u32[]{:S(2)}) collective-permute-start(bf16[128,4,512]{2,0,1:T(8,128)(2,1)S(1)} %get-tuple-element.33), channel_id=1, source_target_pairs={{0,16},{16,32},{32,48},{48,64},{64,80},{80,96},{96,112},{1,17},{17... | collective-permute-start | bytes 1572872 | tf_op jit(solution)/shard_map/ppermute | solution.py:13
  48.7 10.5 %collective-permute-start.2 = (bf16[128,4,512]{2,0,1:T(8,128)(2,1)S(1)}, bf16[128,4,512]{2,0,1:T(8,128)(2,1)S(1)}, u32[]{:S(2)}, u32[]{:S(2)}) collective-permute-start(bf16[128,4,512]{2,0,1:T(8,128)(2,1)S(1)} %get-tuple-element.32), channel_id=1, source_target_pairs={{16,0},{32,16},{48,32},{64,48},{80,64},{96,80},{112,96},{17,1},{33... | collective-permute-start | bytes 1572872 | tf_op jit(solution)/shard_map/ppermute | solution.py:13
  50.6 9.8 %collective-permute-start.3 = (bf16[128,4,512]{2,0,1:T(8,128)(2,1)S(1)}, bf16[128,4,512]{2,0,1:T(8,128)(2,1)S(1)}, u32[]{:S(2)}, u32[]{:S(2)}) collective-permute-start(bf16[128,4,512]{2,0,1:T(8,128)(2,1)S(1)} %get-tuple-element.31), channel_id=1, source_target_pairs={{0,16},{16,32},{32,48},{48,64},{64,80},{80,96},{96,112},{1,17},{17... | collective-permute-start | bytes 1572872 | tf_op jit(solution)/shard_map/ppermute | solution.py:13
  90.0 91.2 %copy-start.4 = (s32[8]{0:T(128)S(1)}, s32[8]{0:T(128)}, u32[]{:S(2)}) copy-start(s32[8]{0:T(128)} %param.11) | copy-start | bytes 100
  90.0 195.1 %all-reduce.4.cloned.1.call-start = ((), (), s32[]{:S(2)}) async-start(), calls=%async_computation.2 | async-start | bytes 8388608 | tf_op jit(solution)/shard_map/psum | solution.py:86
  177.2 7.0 %copy-start.2 = (f32[128,1024]{0,1:T(8,128)S(1)}, f32[128,1024]{0,1:T(8,128)}, u32[]{:S(2)}) copy-start(f32[128,1024]{0,1:T(8,128)} %reduce-scatter.2.cloned.1.call-done) | copy-start | bytes 1572868
  300.3 1.9 copy-start.1
Sparse Core Ops, SparseCore 0:
  90.1 87.0 reduce-scatter.1
  181.3 103.8 all-reduce.3
where the time goes:
time: 650 us; the launch traced here: 640 us
  other arithmetic  277 us (43%)
  waiting for transfers between devices  193 us (30%)
  local copies, waits for them, and re-layouts  74.6 us (11%)
  matrix products  59.6 us (9%)
  between operations  24.2 us (4%)
  starting transfers between devices  12.1 us (2%)
    another operation x31, other arithmetic, per_device(): factor_low = jnp.linalg.cholesky(gram_matrix)  168 us
    psum x1, waiting for transfers between devices, per_device(): gram_matrix = lax.psum(local_gram, 'row')  101 us
    reduce_scatter x1, waiting for transfers between devices, per_device(): lax.psum_scatter(jnp.einsum('prk,lpr->kl', site_tensor, block_rows, prefe...  87.1 us
    another operation x3, other arithmetic, per_device(): jax.scipy.linalg.solve_triangular(factor_low, contracted.astype(jnp.float...  83.6 us
    another operation x14, matrix products, per_device(): factor_low = jnp.linalg.cholesky(gram_matrix)  27 us
    another operation x40, local copies, waits for them, and re-layouts  23.5 us
    dot_general x1, matrix products, per_device(): jnp.einsum('prk,lpr->kl', site_tensor, block_rows, preferred_element_type...  15.6 us
    another operation x15, matrix products, per_device(): jax.scipy.linalg.solve_triangular(factor_low, contracted.astype(jnp.float...  13 us
  transfers between devices with their start and end apart: 6, of which 4 were waited for; matrix products, arithmetic and copies ran while one was open for 3% of the time, Pallas kernels for 0%

commit v1 on v0

--- a/solution.py
+++ b/solution.py
@@ -1,3 +1,4 @@
+import functools
 import math
 import jax
 import jax.numpy as jnp
@@ -5,6 +6,14 @@
 from jax.sharding import PartitionSpec as P
 
 KOUT = 2048
+
+
+def close_point_here(inner_x, which_axis):
+    low = lax.all_gather(inner_x, axis_name=which_axis).sum(axis=0)
+    return low
+
+
+launch_kinds = functools.partial(close_point_here, which_axis="row")
 
 
 def shifted(x, axis, by):
@@ -83,7 +92,7 @@
     local_gram = lax.dot_general(
         contracted, contracted, (((0,), (0,)), ((), ())), preferred_element_type=jnp.float32
     )
-    gram_matrix = lax.psum(local_gram, "row")
+    gram_matrix = launch_kinds(local_gram)
     dead_rows = (row_index >= live_rows).astype(jnp.float32)
     gram_matrix = gram_matrix + jnp.diag(dead_rows)
     factor_low = jnp.linalg.cholesky(gram_matrix)

time: 650 us -> 925 us (1.42)
  waiting for transfers between devices: 193 us -> 458 us
  other arithmetic: 277 us -> 300 us
    all_gather x0 -> x1, waiting for transfers between devices: none -> 366 us  [close_point_here(): low = lax.all_gather(inner_x, axis_name=which_axis).sum(axis=0)]
    psum x1 -> x0, waiting for transfers between devices: 101 us -> none  [per_device(): gram_matrix = lax.psum(local_gram, 'row')]
    reduce_sum x0 -> x1, other arithmetic: none -> 22.9 us  [close_point_here(): low = lax.all_gather(inner_x, axis_name=which_axis).sum(axis=0)]
    another operation x40 -> x24, local copies, waits for them, and re-layouts: 23.5 us -> 22.7 us
  transfers between devices with their start and end apart: 6 -> 6, of which waited for: 4 -> 4; matrix products, arithmetic and copies ran while one was open for 3% -> 2% of each run, Pallas kernels for 0% -> 0%
where the time goes in v1:
time: 925 us; the launch traced here: 916 us
  waiting for transfers between devices  458 us (50%)
  other arithmetic  300 us (32%)
  local copies, waits for them, and re-layouts  67.5 us (7%)
  matrix products  54.2 us (6%)
  between operations  24.2 us (3%)
  starting transfers between devices  12.1 us (1%)
    all_gather x1, waiting for transfers between devices, close_point_here(): low = lax.all_gather(inner_x, axis_name=which_axis).sum(axis=0)  366 us
    another operation x31, other arithmetic, per_device(): factor_low = jnp.linalg.cholesky(gram_matrix)  173 us
    reduce_scatter x1, waiting for transfers between devices, per_device(): lax.psum_scatter(jnp.einsum('prk,lpr->kl', site_tensor, block_rows, prefe...  87.2 us
    another operation x3, other arithmetic, per_device(): jax.scipy.linalg.solve_triangular(factor_low, contracted.astype(jnp.float...  83.6 us
    another operation x14, matrix products, per_device(): factor_low = jnp.linalg.cholesky(gram_matrix)  23.1 us
    reduce_sum x1, other arithmetic, close_point_here(): low = lax.all_gather(inner_x, axis_name=which_axis).sum(axis=0)  22.9 us
    another operation x24, local copies, waits for them, and re-layouts  22.7 us
  transfers between devices with their start and end apart: 6, of which 4 were waited for; matrix products, arithmetic and copies ran while one was open for 2% of the time, Pallas kernels for 0%

profile of v1, /device:TPU:1, one launch (start us, length us, event | category | flops | bytes accessed | tf_op | source)
XLA Modules:
  0.0 916.0 jit_solution(9308460949941286934)
XLA Ops:
  6.5 1.3 dynamic_slice.40
  11.2 3.8 convert_select_fusion
  15.3 3.1 copy-done
  18.4 3.3 collective-permute-start
  21.7 3.2 collective-permute-start.1
  27.6 8.1 concatenate.30
  37.0 1.6 subtract_select_fusion.1
  38.6 5.9 dynamic_update_slice.12
  44.5 2.5 select_dynamic-update-slice_fusion
  47.0 1.9 dynamic-slice_convert_fusion.1
  48.9 1.9 collective-permute-start.2
  50.8 3.6 collective-permute-start.3
  55.8 3.6 collective-permute-done.2
  60.5 2.2 add_select_fusion
  62.7 5.9 dynamic_update_slice.14
  68.7 5.9 dynamic_update_slice.15
  74.6 15.6 %fusion.2 = f32[2048,1024]{0,1:T(8,128)} fusion(bf16[1,4,512,2048]{3,2,1,0:T(8,128)(2,1)} %param.7, f32[1152,4,512]{2,0,1:T(8,128)} %dynamic_update_slice.15), kind=kOutput, calls=%fused_computation.7 | convolution fusion | flops 8589934592 | bytes 20971520 | tf_op jit(solution)/shard_map/prk,lpr->kl/dot_general | solution.py:87
  90.3 87.2 %reduce-scatter.2.cloned.1.call-done = f32[128,1024]{0,1:T(8,128)} async-done(((f32[2048,1024]{0,1:T(8,128)}), f32[128,1024]{0,1:T(8,128)}) %reduce-scatter.2.cloned.1.call-update) | async-done | bytes 524304 | tf_op jit(solution)/shard_map/reduce_scatter | solution.py:86
  177.5 3.9 fusion.45
  184.6 366.2 %all-gather.3.cloned.1.call-done = f32[16384,1024]{1,0:T(8,128)} async-done(((f32[1024,1024]{1,0:T(8,128)}), f32[16384,1024]{1,0:T(8,128)}) %all-gather.3.cloned.1.call-update) | async-done | bytes 67108880 | tf_op jit(solution)/shard_map/all_gather | solution.py:12
  550.9 22.9 %reduce_sum.11 = f32[1024,1024]{1,0:T(8,128)} reduce(f32[16,1024,1024]{2,1,0:T(8,128)} %bitcast.16, f32[]{:T(128)} %constant.290.clone.1), dimensions={0}, to_apply=%region_1.2 | reduce | flops 15728640 | bytes 71303168 | tf_op jit(solution)/shard_map/reduce_sum | solution.py:12
  573.8 5.8 copy.8
  579.6 4.5 add_multiply_fusion
  584.2 1.9 copy-done.1
  586.1 11.7 %cholesky.222 = f32[128,128]{1,0:T(8,128)S(1)} custom-call(f32[128,128]{1,0:T(8,128)S(1)} %cholesky.577), custom_call_target="Cholesky" | custom-call | tf_op jit(solution)/shard_map/jit(cholesky)/cholesky | solution.py:98
  597.8 2.5 cholesky.254
  600.4 9.8 %custom-call.63 = f32[1,128,128]{1,2,0:T(8,128)S(1)} custom-call(f32[1,128,128]{2,1,0:T(8,128)S(1)} %get-tuple-element.77), custom_call_target="InvertDiagBlocksLowerTriangular" | custom-call | tf_op jit(solution)/shard_map/jit(cholesky)/cholesky | solution.py:98
  610.2 2.4 constant_dynamic-update-slice_fusion.25
  612.5 1.5 convolution_subtract_fusion
  614.1 11.8 %cholesky.243 = f32[128,128]{1,0:T(8,128)S(1)} custom-call(f32[128,128]{1,0:T(8,128)S(1)} %cholesky.581), custom_call_target="Cholesky" | custom-call | tf_op jit(solution)/shard_map/jit(cholesky)/cholesky | solution.py:98
  627.9 9.8 %custom-call.64 = f32[1,128,128]{1,2,0:T(8,128)S(1)} custom-call(f32[1,128,128]{2,1,0:T(8,128)S(1)} %get-tuple-element.74), custom_call_target="InvertDiagBlocksLowerTriangular" | custom-call | tf_op jit(solution)/shard_map/jit(cholesky)/cholesky | solution.py:98
  637.7 1.2 convolution_dynamic-update-slice_fusion
  638.9 2.1 convolution_subtract_fusion.1
  641.0 11.7 %cholesky.466 = f32[128,128]{1,0:T(8,128)S(1)} custom-call(f32[128,128]{1,0:T(8,128)S(1)} %cholesky.586), custom_call_target="Cholesky" | custom-call | tf_op jit(solution)/shard_map/jit(cholesky)/cholesky | solution.py:98
  654.0 9.8 %custom-call.65 = f32[1,128,128]{1,2,0:T(8,128)S(1)} custom-call(f32[1,128,128]{2,1,0:T(8,128)S(1)} %get-tuple-element.71), custom_call_target="InvertDiagBlocksLowerTriangular" | custom-call | tf_op jit(solution)/shard_map/jit(cholesky)/cholesky | solution.py:98
  665.0 2.3 convolution_subtract_fusion.2
  667.4 11.9 %cholesky.485 = f32[128,128]{1,0:T(8,128)S(1)} custom-call(f32[128,128]{1,0:T(8,128)S(1)} %cholesky.591), custom_call_target="Cholesky" | custom-call | tf_op jit(solution)/shard_map/jit(cholesky)/cholesky | solution.py:98
  680.6 9.8 %custom-call.66 = f32[1,128,128]{1,2,0:T(8,128)S(1)} custom-call(f32[1,128,128]{2,1,0:T(8,128)S(1)} %get-tuple-element.68), custom_call_target="InvertDiagBlocksLowerTriangular" | custom-call | tf_op jit(solution)/shard_map/jit(cholesky)/cholesky | solution.py:98
  691.5 2.3 convolution_subtract_fusion.3
  693.8 11.7 %cholesky.504 = f32[128,128]{1,0:T(8,128)S(1)} custom-call(f32[128,128]{1,0:T(8,128)S(1)} %cholesky.596), custom_call_target="Cholesky" | custom-call | tf_op jit(solution)/shard_map/jit(cholesky)/cholesky | solution.py:98
  706.8 10.2 %custom-call.67 = f32[1,128,128]{1,2,0:T(8,128)S(1)} custom-call(f32[1,128,128]{2,1,0:T(8,128)S(1)} %get-tuple-element.65), custom_call_target="InvertDiagBlocksLowerTriangular" | custom-call | tf_op jit(solution)/shard_map/jit(cholesky)/cholesky | solution.py:98
  718.0 2.3 convolution_subtract_fusion.4
  720.3 11.7 %cholesky.524 = f32[128,128]{1,0:T(8,128)S(1)} custom-call(f32[128,128]{1,0:T(8,128)S(1)} %cholesky.601), custom_call_target="Cholesky" | custom-call | tf_op jit(solution)/shard_map/jit(cholesky)/cholesky | solution.py:98
  733.3 9.8 %custom-call.68 = f32[1,128,128]{1,2,0:T(8,128)S(1)} custom-call(f32[1,128,128]{2,1,0:T(8,128)S(1)} %get-tuple-element.62), custom_call_target="InvertDiagBlocksLowerTriangular" | custom-call | tf_op jit(solution)/shard_map/jit(cholesky)/cholesky | solution.py:98
  744.1 2.0 convolution_subtract_fusion.5
  746.1 11.9 %cholesky.544 = f32[128,128]{1,0:T(8,128)S(1)} custom-call(f32[128,128]{1,0:T(8,128)S(1)} %cholesky.606), custom_call_target="Cholesky" | custom-call | tf_op jit(solution)/shard_map/jit(cholesky)/cholesky | solution.py:98
  759.3 9.8 %custom-call.69 = f32[1,128,128]{1,2,0:T(8,128)S(1)} custom-call(f32[1,128,128]{2,1,0:T(8,128)S(1)} %get-tuple-element.59), custom_call_target="InvertDiagBlocksLowerTriangular" | custom-call | tf_op jit(solution)/shard_map/jit(cholesky)/cholesky | solution.py:98
  770.0 1.8 convolution_subtract_fusion.11
  771.8 11.7 %cholesky.562 = f32[128,128]{1,0:T(8,128)S(1)} custom-call(f32[128,128]{1,0:T(8,128)S(1)} %convolution_subtract_fusion.11), custom_call_target="Cholesky" | custom-call | tf_op jit(solution)/shard_map/jit(cholesky)/cholesky | solution.py:98
  789.8 4.8 select_select_fusion
  794.6 22.8 %while.1 = (s32[]{:T(128)}, f32[1024,1024]{1,0:T(8,128)}, s32[8,2]{0,1:T(2,128)S(1)}, f32[8,128,128]{2,1,0:T(8,128)S(1)}, s32[]{:T(128)}) while((s32[]{:T(128)}, f32[1024,1024]{1,0:T(8,128)}, s32[8,2]{0,1:T(2,128)S(1)}, f32[8,128,128]{2,1,0:T(8,128)S(1)}, s32[]{:T(128)}) %tuple.72), condition=%wide.while_cond, body=%wide.while_body.sunk | while | flops 2 | bytes 131181 | solution.py:99
  795.2 2.2 bitcast_dynamic-update-slice_fusion.2
  798.0 2.2 bitcast_dynamic-update-slice_fusion.2
  800.9 2.2 bitcast_dynamic-update-slice_fusion.2
  803.8 2.2 bitcast_dynamic-update-slice_fusion.2
  806.6 2.2 bitcast_dynamic-update-slice_fusion.2
  809.5 2.2 bitcast_dynamic-update-slice_fusion.2
  812.4 2.2 bitcast_dynamic-update-slice_fusion.2
  815.2 2.2 bitcast_dynamic-update-slice_fusion.2
  817.4 78.8 %custom-call.70 = f32[8,128,128]{1,2,0:T(8,128)S(1)} custom-call(f32[8,128,128]{2,1,0:T(8,128)S(1)} %get-tuple-element.12), custom_call_target="InvertDiagBlocksLowerTriangular" | custom-call | tf_op jit(solution)/shard_map/jit(_solve_triangular)/triangular_solve | solution.py:99
  900.8 1.3 convolution_subtract_fusion.12
  902.5 1.4 convolution_subtract_fusion.8
  904.2 1.5 convolution_subtract_fusion.7
  906.0 1.6 convolution_subtract_fusion.6
  (90 shorter events, 34.8 us)
Async XLA Ops:
  6.5 170.9 %reduce-scatter.2.cloned.1.call-start = ((), (), s32[]{:S(2)}) async-start(), calls=%async_computation.1 | async-start | bytes 8912896 | tf_op jit(solution)/shard_map/reduce_scatter | solution.py:86
  15.1 3.3 copy-start
  15.1 9.8 %copy-start.3 = (f32[2,8,128]{2,1,0:T(8,128)S(1)}, f32[2,8,128]{2,1,0:T(8,128)}, u32[]{:S(2)}) copy-start(f32[2,8,128]{2,1,0:T(8,128)} %param.10) | copy-start | bytes 24580
  18.4 18.6 %collective-permute-start = (bf16[128,4,512]{2,0,1:T(8,128)(2,1)S(1)}, bf16[128,4,512]{2,0,1:T(8,128)(2,1)S(1)}, u32[]{:S(2)}, u32[]{:S(2)}) collective-permute-start(bf16[128,4,512]{2,0,1:T(8,128)(2,1)S(1)} %get-tuple-element.30), channel_id=1, source_target_pairs={{16,0},{32,16},{48,32},{64,48},{80,64},{96,80},{112,96},{17,1},{33... | collective-permute-start | bytes 1572872 | tf_op jit(solution)/shard_map/ppermute | solution.py:22
  21.7 22.8 %collective-permute-start.1 = (bf16[128,4,512]{2,0,1:T(8,128)(2,1)S(1)}, bf16[128,4,512]{2,0,1:T(8,128)(2,1)S(1)}, u32[]{:S(2)}, u32[]{:S(2)}) collective-permute-start(bf16[128,4,512]{2,0,1:T(8,128)(2,1)S(1)} %get-tuple-element.29), channel_id=1, source_target_pairs={{0,16},{16,32},{32,48},{48,64},{64,80},{80,96},{96,112},{1,17},{17... | collective-permute-start | bytes 1572872 | tf_op jit(solution)/shard_map/ppermute | solution.py:22
  48.9 10.5 %collective-permute-start.2 = (bf16[128,4,512]{2,0,1:T(8,128)(2,1)S(1)}, bf16[128,4,512]{2,0,1:T(8,128)(2,1)S(1)}, u32[]{:S(2)}, u32[]{:S(2)}) collective-permute-start(bf16[128,4,512]{2,0,1:T(8,128)(2,1)S(1)} %get-tuple-element.28), channel_id=1, source_target_pairs={{16,0},{32,16},{48,32},{64,48},{80,64},{96,80},{112,96},{17,1},{33... | collective-permute-start | bytes 1572872 | tf_op jit(solution)/shard_map/ppermute | solution.py:22
  50.8 9.8 %collective-permute-start.3 = (bf16[128,4,512]{2,0,1:T(8,128)(2,1)S(1)}, bf16[128,4,512]{2,0,1:T(8,128)(2,1)S(1)}, u32[]{:S(2)}, u32[]{:S(2)}) collective-permute-start(bf16[128,4,512]{2,0,1:T(8,128)(2,1)S(1)} %get-tuple-element.27), channel_id=1, source_target_pairs={{0,16},{16,32},{32,48},{48,64},{64,80},{80,96},{96,112},{1,17},{17... | collective-permute-start | bytes 1572872 | tf_op jit(solution)/shard_map/ppermute | solution.py:22
  90.2 91.2 %copy-start.4 = (s32[8]{0:T(128)S(1)}, s32[8]{0:T(128)}, u32[]{:S(2)}) copy-start(s32[8]{0:T(128)} %param.11) | copy-start | bytes 100
  90.2 460.7 %all-gather.3.cloned.1.call-start = ((), (), s32[]{:S(2)}) async-start(), calls=%async_computation.2 | async-start | bytes 71303168 | tf_op jit(solution)/shard_map/all_gather | solution.py:12
  177.5 7.1 copy-start.2
  584.2 1.9 copy-start.1
Sparse Core Ops, SparseCore 0:
  90.3 87.0 reduce-scatter.1
  181.6 369.2 all-gather.2
